TPU v7x, 32 devices: a whole 2x2x4 slice. The times are simulated.
32 devices in a mesh: grp: 4 (over y, core), shard: 8 (over z, x).
Axes of the slice: x: 2, y: 2, z: 4, core: 2. Of those that a mesh axis runs over, the one named last changes fastest.
Arguments:
- query_rows: bfloat16 [16, 6144], P('grp'), may hold values from -10 to 10
- key_cache: bfloat16 [16, 2048, 1024], P('grp', 'shard'), may hold values from -10 to 10
- value_cache: bfloat16 [16, 2048, 1024], P('grp', 'shard'), may hold values from -6 to 6
- lengths: int32 [16], P('grp'), may hold values from 2 to 2048
- attn_gain: float32 [6144], replicated, may hold values from 0.5 to 1.5
- router: bfloat16 [6144, 4], replicated, may hold values from -0.078125 to 0.078125
- expert_ids: int32 [16, 2], replicated, may hold values from 0 to 3, all different within a row; in each aligned block of 4 rows (0 to 3, 4 to 7, ...) at most 2 rows name the same one
- w_gate: bfloat16 [4, 6144, 8192], P('grp', None, 'shard'), may hold values from -0.078125 to 0.078125
- w_up: bfloat16 [4, 6144, 8192], P('grp', None, 'shard'), may hold values from -0.078125 to 0.078125
- w_down: bfloat16 [4, 8192, 6144], P('grp', 'shard'), may hold values from -0.0625 to 0.0625
Outputs:
- normed: bfloat16 [16, 6144], P('grp')
- expert_out: bfloat16 [16, 6144], P('grp', 'shard')
Inputs may be any that keep to these rules, and one draw needn't show every extreme that they name: `expert_ids`: the two ids of a row differ. Among the 4 rows of one index of grp (aligned blocks), no expert is named by more than 2 rows, a bound that some block reaches.
All inputs are finite; a program needn't handle non-finite values.
Results may differ from a plain program's by a relative error of at most 0.0095.
Values may be sent and summed in bfloat16 or wider, within the bound.
No kernel may reach another device: no remote copies, remote signals or barrier semaphores. Data moves between devices by JAX's collectives and lax.ppermute only.
A program may use at most 128 MiB of HBM per device.

v0:
```python
import math
import jax
import jax.numpy as jnp
from jax import lax
from jax.sharding import PartitionSpec as P

HEADS = 48
KV_HEADS = 8
HEAD_DIM = 128
NEG_FILL = -1e30


def combined_all(value, axis, join):
    pieces = jax.tree.map(lambda part: lax.all_gather(part, axis), value)
    head = jax.tree.map(lambda part: part[0], pieces)
    tail = jax.tree.map(lambda part: part[1:], pieces)
    total, _ = lax.scan(lambda total, share: (join(total, share), None), head, tail)
    return total


def merge_parts(earlier, second):
    joint_max = jnp.maximum(earlier[0], second[0])
    left_scale = jnp.exp(earlier[0] - joint_max)
    right_scale = jnp.exp(second[0] - joint_max)
    joint_sum = earlier[1] * left_scale + second[1] * right_scale
    joint_mix = earlier[2] * left_scale[..., None] + second[2] * right_scale[..., None]
    return (joint_max, joint_sum, joint_mix)


def shards(
    query_rows, key_cache, value_cache, lengths, attn_gain, router, expert_ids, w_gate, w_up, w_down
):
    rows_here = query_rows.shape[0]
    span = key_cache.shape[1]
    kv_share = HEADS // KV_HEADS
    shard_id = lax.axis_index("shard")
    query_heads = query_rows.reshape(rows_here, KV_HEADS, kv_share, HEAD_DIM)
    key_heads = key_cache.reshape(rows_here, span, KV_HEADS, HEAD_DIM)
    value_heads = value_cache.reshape(rows_here, span, KV_HEADS, HEAD_DIM)
    scores = jnp.einsum(
        "rgjd,rtgd->rgjt", query_heads, key_heads, preferred_element_type=jnp.float32
    ) / math.sqrt(HEAD_DIM)
    position = shard_id * span + jnp.arange(span, dtype=jnp.int32)
    live_mask = (position[None, :] < lengths[:, None])[:, None, None, :]
    scores = jnp.where(live_mask, scores, NEG_FILL)
    block_max = jnp.max(scores, axis=-1)
    block_probs = jnp.where(live_mask, jnp.exp(scores - block_max[..., None]), 0.0).astype(
        jnp.bfloat16
    )
    block_sum = jnp.sum(block_probs.astype(jnp.float32), axis=-1)
    block_mix = jnp.einsum(
        "rgjt,rtgd->rgjd", block_probs, value_heads, preferred_element_type=jnp.float32
    )
    whole_max, whole_sum, whole_mix = combined_all(
        (block_max, block_sum, block_mix), "shard", merge_parts
    )
    attended = (whole_mix / whole_sum[..., None]).reshape(rows_here, -1)
    mean_square = jnp.mean(attended * attended, axis=-1, keepdims=True)
    normed = (attended * lax.rsqrt(mean_square + 1e-05) * attn_gain).astype(jnp.bfloat16)
    experts = router.shape[1]
    capacity = rows_here // 2
    width = normed.shape[1]
    logits = jnp.dot(normed, router, preferred_element_type=jnp.float32)
    own_ids = lax.dynamic_slice_in_dim(expert_ids, lax.axis_index("grp") * rows_here, rows_here, 0)
    expert_range = jnp.arange(experts, dtype=jnp.int32)
    expert_hit = own_ids[:, :, None] == expert_range[None, None, :]
    chosen = jnp.sum(jnp.where(expert_hit, logits[:, None, :], 0.0), axis=-1)
    first_weight = jax.nn.sigmoid(chosen[:, 0] - chosen[:, 1])
    route_weight = jnp.stack([first_weight, 1.0 - first_weight], axis=1)
    row_range = jnp.arange(rows_here, dtype=jnp.int32)
    strictly_lower = (row_range[:, None] > row_range[None, :]).astype(jnp.float32)
    counts = jnp.sum(expert_hit, axis=1).astype(jnp.float32)
    before = jnp.dot(
        strictly_lower, counts, precision=lax.Precision.HIGHEST, preferred_element_type=jnp.float32
    )
    slot_index = jnp.sum(jnp.where(expert_hit, before[:, None, :], 0.0), axis=-1)
    slot_base = jnp.sum(
        jnp.where(expert_hit, (expert_range * capacity).astype(jnp.float32)[None, None, :], 0.0),
        axis=-1,
    )
    destination = slot_base + slot_index
    slot_columns = jnp.arange(experts * capacity, dtype=jnp.int32).astype(jnp.float32)
    placed = (destination[:, :, None] == slot_columns[None, None, :]).astype(jnp.float32)
    send_matrix = jnp.sum(placed, axis=1)
    combine_matrix = jnp.sum(placed * route_weight[:, :, None], axis=1)
    gate_local = w_gate[0]
    up_local = w_up[0]
    down_local = w_down[0]
    outgoing = jnp.einsum(
        "rc,rd->cd", send_matrix.astype(jnp.bfloat16), normed, preferred_element_type=jnp.float32
    )
    outgoing = outgoing.astype(jnp.bfloat16).reshape(experts, capacity, width)
    arrived = lax.all_to_all(outgoing, "grp", split_axis=0, concat_axis=0, tiled=True)
    gate_proj = jnp.einsum("gcd,df->gcf", arrived, gate_local, preferred_element_type=jnp.float32)
    up_proj = jnp.einsum("gcd,df->gcf", arrived, up_local, preferred_element_type=jnp.float32)
    hidden = (jax.nn.silu(gate_proj) * up_proj).astype(jnp.bfloat16)
    partial_value = jnp.einsum(
        "gcf,fd->gcd", hidden, down_local, preferred_element_type=jnp.float32
    )
    summed = lax.psum(partial_value, "shard")
    returned = lax.all_to_all(summed, "grp", split_axis=0, concat_axis=0, tiled=True)
    full_rows = jnp.dot(
        combine_matrix,
        returned.reshape(experts * capacity, width),
        precision=lax.Precision.HIGHEST,
        preferred_element_type=jnp.float32,
    )
    out_width = width // lax.axis_size("shard")
    result = lax.dynamic_slice_in_dim(full_rows, shard_id * out_width, out_width, 1)
    return (normed, result.astype(jnp.bfloat16))


def solution(mesh):
    in_specs = (
        P("grp", None),
        P("grp", "shard", None),
        P("grp", "shard", None),
        P("grp"),
        P(),
        P(),
        P(),
        P("grp", None, "shard"),
        P("grp", None, "shard"),
        P("grp", "shard", None),
    )
    out_specs = (P("grp", None), P("grp", "shard"))
    return jax.shard_map(shards, mesh=mesh, in_specs=in_specs, out_specs=out_specs, check_vma=False)
```

profile of v0, /device:TPU:0, one launch (start us, length us, event | category | flops | bytes accessed | tf_op | source)
XLA Modules:
  0.0 222.4 jit_solution(8904298598831475986)
XLA Ops:
  7.3 1.0 reshape.80
  8.3 0.9 broadcast_compare_fusion
  9.2 0.7 fusion.36
  9.9 32.4 %all-gather = f32[32,8,6]{2,1,0:T(8,128)S(1)} all-gather(f32[4,8,6]{2,1,0:T(8,128)S(1)} %get-tuple-element.90), channel_id=2, replica_groups=mesh['grp'=4,'shard'=8] {'shard'}, dimensions={0}, use_global_device_ids=true | all-gather | bytes 6912 | tf_op jit(solution)/shard_map/all_gather | solution.py:14
  42.3 0.2 convert_reduce_fusion
  42.5 30.5 %all-gather.1 = f32[32,8,6]{2,1,0:T(8,128)S(1)} all-gather(f32[4,8,6]{2,1,0:T(8,128)S(1)} %convert_reduce_fusion), channel_id=3, replica_groups=mesh['grp'=4,'shard'=8] {'shard'}, dimensions={0}, use_global_device_ids=true | all-gather | bytes 6912 | tf_op jit(solution)/shard_map/all_gather | solution.py:14
  73.1 0.4 fusion.10
  73.5 31.6 %all-gather.2 = f32[32,8,6,128]{3,1,2,0:T(8,128)S(1)} all-gather(f32[4,8,6,128]{3,1,2,0:T(8,128)S(1)} %copy.53), channel_id=4, replica_groups=mesh['grp'=4,'shard'=8] {'shard'}, dimensions={0}, use_global_device_ids=true | all-gather | bytes 884736 | tf_op jit(solution)/shard_map/all_gather | solution.py:14
  105.6 0.2 copy.59
  105.9 0.2 copy.60
  106.3 3.0 %while.14 = (s32[]{:T(128)}, f32[4,8,6]{1,0,2:T(4,128)S(1)}, f32[4,8,6]{1,0,2:T(4,128)S(1)}, f32[4,8,6,128]{3,2,1,0:T(8,128)S(1)}, f32[7,4,8,6]{2,1,3,0:T(4,128)...) while((s32[]{:T(128)}, f32[4,8,6]{1,0,2:T(4,128)S(1)}, ...), condition=%wide.region_3.4_spmd, body=%wide.region_2.3_spmd.sunk | while | flops 74882 | bytes 502373 | solution.py:17
  109.3 0.2 multiply_reduce_fusion
  109.9 0.2 select_reduce_fusion.1
  110.2 0.2 convolution_convert_fusion
  110.5 6.9 %all_to_all.10 = bf16[4,2,6144]{2,1,0:T(2,128)(2,1)S(1)} all-to-all(bf16[4,2,6144]{2,1,0:T(2,128)(2,1)S(1)} %reshape.84), channel_id=1, replica_groups=mesh['grp'=4,'shard'=8] {'grp'}, dimensions={0} | all-to-all | bytes 196608 | tf_op jit(solution)/shard_map/all_to_all | solution.py:93
  117.4 6.8 %fusion.8 = f32[4,2,1024]{2,1,0:T(2,128)S(1)} fusion(bf16[4,2,6144]{2,1,0:T(2,128)(2,1)S(1)} %all_to_all.10, bf16[1,6144,1024]{2,1,0:T(8,128)(2,1)} %param.19), kind=kOutput, calls=%fused_computation.14 | convolution fusion | flops 100663296 | bytes 12713984 | tf_op jit(solution)/shard_map/gcd,df->gcf/dot_general | solution.py:94
  124.2 6.7 %fusion.25 = bf16[4,2,1024]{2,1,0:T(2,128)(2,1)S(1)} fusion(bf16[4,2,6144]{2,1,0:T(2,128)(2,1)S(1)} %all_to_all.10, bf16[1,6144,1024]{2,1,0:T(8,128)(2,1)} %param.20, f32[4,2,1024]{2,1,0:T(2,128)S(1)} %fusion.8), kind=kOutput, calls=%fused_computation.26 | convolution fusion | flops 100712448 | bytes 12730368 | tf_op jit(solution)/shard_map/gcd,df->gcf/dot_general | solution.py:95
  130.9 2.5 %fusion.4 = f32[4,2,6144]{2,0,1:T(4,128)} fusion(bf16[1,1024,6144]{2,1,0:T(8,128)(2,1)S(1)} %bitcast.70, bf16[4,2,1024]{2,1,0:T(2,128)(2,1)S(1)} %fusion.25), kind=kOutput, calls=%fused_computation.10 | convolution fusion | flops 100663296 | bytes 12795904 | tf_op jit(solution)/shard_map/gcf,fd->gcd/dot_general | solution.py:97
  133.5 70.6 %all-reduce.2.cloned.1.call-done = f32[4,2,6144]{2,0,1:T(4,128)} async-done(((f32[4,2,6144]{2,0,1:T(4,128)}), f32[4,2,6144]{2,0,1:T(4,128)}) %all-reduce.2.cloned.1.call-update) | async-done | bytes 196624 | tf_op jit(solution)/shard_map/psum | solution.py:100
  204.1 1.8 copy.64
  205.8 3.4 %all-to-all-start.1 = ((f32[4,2,6144]{2,1,0:T(2,128)}), f32[4,2,6144]{2,1,0:T(2,128)S(1)}, u32[]{:S(2)}, u32[]{:S(2)}) async-start(f32[4,2,6144]{2,1,0:T(2,128)} %copy.64), calls=%async_computation.1 | async-start | bytes 393216 | tf_op jit(solution)/shard_map/all_to_all | solution.py:101
  209.2 5.3 %all-to-all-done.1 = f32[4,2,6144]{2,1,0:T(2,128)S(1)} async-done(((f32[4,2,6144]{2,1,0:T(2,128)}), f32[4,2,6144]{2,1,0:T(2,128)S(1)}, u32[]{:S(2)}, u32[]{:S(2)}) %all-to-all-start.1) | async-done | bytes 196640 | tf_op jit(solution)/shard_map/all_to_all | solution.py:101
  214.6 0.3 fusion.38
  214.9 0.6 dynamic-slice_convert_fusion
  (83 shorter events, 4.3 us)
Async XLA Ops:
  7.2 2.0 copy-start
  7.2 196.9 %all-reduce.2.cloned.1.call-start = ((), (), s32[]{:S(2)}) async-start(), calls=%async_computation.2 | async-start | bytes 393216 | tf_op jit(solution)/shard_map/psum | solution.py:100
  8.3 64.8 %copy-start.1 = (bf16[4,256,1024]{2,1,0:T(8,128)(2,1)S(1)}, bf16[4,256,1024]{2,1,0:T(8,128)(2,1)}, u32[]{:S(2)}) copy-start(bf16[4,256,1024]{2,1,0:T(8,128)(2,1)} %param.14) | copy-start | bytes 6291460
  73.0 32.2 %copy-start.4 = (s32[16,2]{0,1:T(2,128)S(1)}, s32[16,2]{0,1:T(2,128)}, u32[]{:S(2)}) copy-start(s32[16,2]{0,1:T(2,128)} %param.18) | copy-start | bytes 388
  106.3 3.4 %copy-start.3 = (f32[6144]{0:T(1024)S(1)}, f32[6144]{0:T(1024)}, u32[]{:S(2)}) copy-start(f32[6144]{0:T(1024)} %param.16) | copy-start | bytes 73732
  106.3 3.5 %copy-start.5 = (bf16[6144,4]{0,1:T(4,128)(2,1)S(1)}, bf16[6144,4]{0,1:T(4,128)(2,1)}, u32[]{:S(2)}) copy-start(bf16[6144,4]{0,1:T(4,128)(2,1)} %param.17) | copy-start | bytes 147460
  109.7 14.4 %copy-start.2 = (bf16[4,6144]{1,0:T(4,128)(2,1)}, bf16[4,6144]{1,0:T(4,128)(2,1)S(1)}, u32[]{:S(2)}) copy-start(bf16[4,6144]{1,0:T(4,128)(2,1)S(1)} %multiply_convert_fusion) | copy-start | bytes 147460
  117.4 13.5 %slice-start = ((s8[12582912]{0:T(1024)(128)(4,1)}), s8[4194304]{0:T(1024)(128)(4,1)S(1)}, s32[]{:S(2)}) async-start(s8[12582912]{0:T(1024)(128)(4,1)} %bitcast.69), calls=%async_computation.3 | async-start | bytes 8388608
  117.4 13.5 %slice-start.1 = ((s8[12582912]{0:T(1024)(128)(4,1)}), s8[4194304]{0:T(1024)(128)(4,1)S(1)}, s32[]{:S(2)}) async-start(s8[12582912]{0:T(1024)(128)(4,1)} %bitcast.69), calls=%async_computation.4 | async-start | bytes 8388608
  124.2 6.7 %slice-start.2 = ((s8[12582912]{0:T(1024)(128)(4,1)}), s8[4194304]{0:T(1024)(128)(4,1)S(1)}, s32[]{:S(2)}) async-start(s8[12582912]{0:T(1024)(128)(4,1)} %bitcast.69), calls=%async_computation.5 | async-start | bytes 8388608
  205.8 8.7 %all-to-all-start.1 = ((f32[4,2,6144]{2,1,0:T(2,128)}), f32[4,2,6144]{2,1,0:T(2,128)S(1)}, u32[]{:S(2)}, u32[]{:S(2)}) async-start(f32[4,2,6144]{2,1,0:T(2,128)} %copy.64), calls=%async_computation.1 | async-start | bytes 393216 | tf_op jit(solution)/shard_map/all_to_all | solution.py:101
Sparse Core Ops, SparseCore 0:
  133.6 70.4 all-reduce.1
where the time goes:
time: 223 us; the launch traced here: 222 us
  blocking collectives  101 us (45%)
  waiting for transfers between devices  75.9 us (34%)
  matrix products  17.9 us (8%)
  between operations  14.3 us (6%)
  local copies, waits for them, and re-layouts  6.13 us (3%)
  starting transfers between devices  3.4 us (2%)
  other arithmetic  3.13 us (1%)
    all_gather x3, blocking collectives, combined_all(): pieces = jax.tree.map(lambda part: lax.all_gather(part, axis), value)  94.5 us
    psum x1, waiting for transfers between devices, shards(): summed = lax.psum(partial_value, 'shard')  70.6 us
    all_to_all x1, blocking collectives, shards(): lax.all_to_all(outgoing, 'grp', split_axis=0, concat_axis=0, tiled=True)  6.89 us
    dot_general x1, matrix products, shards(): jnp.einsum('gcd,df->gcf', arrived, gate_local, preferred_element_type=jnp...  6.76 us
    dot_general x1, matrix products, shards(): jnp.einsum('gcd,df->gcf', arrived, up_local, preferred_element_type=jnp.f...  6.69 us
    all_to_all x1, waiting for transfers between devices, shards(): lax.all_to_all(summed, 'grp', split_axis=0, concat_axis=0, tiled=True)  5.29 us
  transfers between devices with their start and end apart: 2, of which 2 were waited for; matrix products, arithmetic and copies ran while one was open for 0% of the time, Pallas kernels for 0%

commit v1 on v0

--- a/solution.py
+++ b/solution.py
@@ -8,6 +8,12 @@
 KV_HEADS = 8
 HEAD_DIM = 128
 NEG_FILL = -1e30
+
+
+def gather_and_add(x, name):
+    parts = lax.all_gather(x, name, axis=0, tiled=False)
+    result = parts.sum(axis=0)
+    return result
 
 
 def combined_all(value, axis, join):
@@ -97,7 +103,7 @@
     partial_value = jnp.einsum(
         "gcf,fd->gcd", hidden, down_local, preferred_element_type=jnp.float32
     )
-    summed = lax.psum(partial_value, "shard")
+    summed = gather_and_add(partial_value, "shard")
     returned = lax.all_to_all(summed, "grp", split_axis=0, concat_axis=0, tiled=True)
     full_rows = jnp.dot(
         combine_matrix,

time: 223 us -> 201 us (0.901)
  waiting for transfers between devices: 75.9 us -> 50.1 us
  matrix products: 17.9 us -> 21 us
  other arithmetic: 3.13 us -> 5.89 us
    psum x1 -> x0, waiting for transfers between devices: 70.6 us -> none  [shards(): summed = lax.psum(partial_value, 'shard')]
    all_gather x0 -> x1, waiting for transfers between devices: none -> 44.8 us  [gather_and_add(): parts = lax.all_gather(x, name, axis=0, tiled=False)]
    dot_general x1, matrix products: 2.5 us -> 12.5 us  [shards(): jnp.einsum('gcf,fd->gcd', hidden, down_local, preferred_element_type=jnp....]
    dot_general x1 -> x0, matrix products: 6.69 us -> none  [shards(): jnp.einsum('gcd,df->gcf', arrived, up_local, preferred_element_type=jnp.f...]
    reduce_sum x0 -> x1, other arithmetic: none -> 2.76 us  [gather_and_add(): result = parts.sum(axis=0)]
where the time goes in v1:
time: 201 us
  blocking collectives  101 us (50%)
  waiting for transfers between devices  50.1 us (25%)
  matrix products  21 us (10%)
  between operations  14.3 us (7%)
  other arithmetic  5.89 us (3%)
  local copies, waits for them, and re-layouts  4.35 us (2%)
  starting transfers between devices  3.4 us (2%)
    all_gather x3, blocking collectives, combined_all(): pieces = jax.tree.map(lambda part: lax.all_gather(part, axis), value)  94.5 us
    all_gather x1, waiting for transfers between devices, gather_and_add(): parts = lax.all_gather(x, name, axis=0, tiled=False)  44.8 us
    dot_general x1, matrix products, shards(): jnp.einsum('gcf,fd->gcd', hidden, down_local, preferred_element_type=jnp....  12.5 us
    all_to_all x1, blocking collectives, shards(): lax.all_to_all(outgoing, 'grp', split_axis=0, concat_axis=0, tiled=True)  6.89 us
    dot_general x1, matrix products, shards(): jnp.einsum('gcd,df->gcf', arrived, gate_local, preferred_element_type=jnp...  6.53 us
    all_to_all x1, waiting for transfers between devices, shards(): lax.all_to_all(summed, 'grp', split_axis=0, concat_axis=0, tiled=True)  5.29 us
  transfers between devices with their start and end apart: 2, of which 2 were waited for; matrix products, arithmetic and copies ran while one was open for 0% of the time, Pallas kernels for 0%

profile of v1, /device:TPU:0, one launch (start us, length us, event | category | flops | bytes accessed | tf_op | source)
XLA Modules:
  0.0 200.7 jit_solution(14880913598832021265)
XLA Ops:
  7.3 1.0 reshape.80
  8.3 0.9 broadcast_compare_fusion
  9.2 0.7 fusion.42
  9.9 32.4 %all-gather = f32[32,8,6]{2,1,0:T(8,128)S(1)} all-gather(f32[4,8,6]{2,1,0:T(8,128)S(1)} %get-tuple-element.104), channel_id=2, replica_groups=mesh['grp'=4,'shard'=8] {'shard'}, dimensions={0}, use_global_device_ids=true | all-gather | bytes 6912 | tf_op jit(solution)/shard_map/all_gather | solution.py:20
  42.3 0.2 convert_reduce_fusion
  42.5 30.5 %all-gather.1 = f32[32,8,6]{2,1,0:T(8,128)S(1)} all-gather(f32[4,8,6]{2,1,0:T(8,128)S(1)} %convert_reduce_fusion), channel_id=3, replica_groups=mesh['grp'=4,'shard'=8] {'shard'}, dimensions={0}, use_global_device_ids=true | all-gather | bytes 6912 | tf_op jit(solution)/shard_map/all_gather | solution.py:20
  73.1 0.4 fusion.10
  73.5 31.6 %all-gather.2 = f32[32,8,6,128]{3,1,2,0:T(8,128)S(1)} all-gather(f32[4,8,6,128]{3,1,2,0:T(8,128)S(1)} %copy.91), channel_id=4, replica_groups=mesh['grp'=4,'shard'=8] {'shard'}, dimensions={0}, use_global_device_ids=true | all-gather | bytes 884736 | tf_op jit(solution)/shard_map/all_gather | solution.py:20
  105.6 0.2 copy.97
  106.0 0.2 copy.98
  106.3 3.0 %while.14 = (s32[]{:T(128)}, f32[4,8,6]{1,0,2:T(4,128)S(1)}, f32[4,8,6]{1,0,2:T(4,128)S(1)}, f32[4,8,6,128]{3,2,1,0:T(8,128)S(1)}, f32[7,4,8,6]{2,1,3,0:T(4,128)...) while((s32[]{:T(128)}, f32[4,8,6]{1,0,2:T(4,128)S(1)}, ...), condition=%wide.region_3.4_spmd, body=%wide.region_2.3_spmd.sunk | while | flops 74882 | bytes 502373 | solution.py:23
  106.5 0.2 fusion.59
  109.4 0.2 multiply_reduce_fusion
  109.9 0.2 select_reduce_fusion.1
  110.2 0.2 convolution_convert_fusion
  110.5 6.9 %all_to_all.10 = bf16[4,2,6144]{2,1,0:T(2,128)(2,1)S(1)} all-to-all(bf16[4,2,6144]{2,1,0:T(2,128)(2,1)S(1)} %reshape.84), channel_id=1, replica_groups=mesh['grp'=4,'shard'=8] {'grp'}, dimensions={0} | all-to-all | bytes 196608 | tf_op jit(solution)/shard_map/all_to_all | solution.py:99
  117.4 6.5 %fusion.8 = f32[4,2,1024]{2,1,0:T(2,128)S(1)} fusion(bf16[4,2,6144]{2,1,0:T(2,128)(2,1)S(1)} %all_to_all.10, bf16[1,6144,1024]{2,1,0:T(8,128)(2,1)} %param.19), kind=kOutput, calls=%fused_computation.14 | convolution fusion | flops 100663296 | bytes 12713984 | tf_op jit(solution)/shard_map/gcd,df->gcf/dot_general | solution.py:100
  124.0 12.5 %fusion.4 = f32[4,2,6144]{2,1,0:T(2,128)} fusion(bf16[1,1024,6144]{2,1,0:T(8,128)(2,1)} %param.21, bf16[4,2,6144]{2,1,0:T(2,128)(2,1)S(1)} %all_to_all.10, bf16[1,6144,1024]{2,1,0:T(8,128)(2,1)} %param.20, f32[4,2,1024]{2,1,0:T(2,128)S(1)} %fusion.8), kind=kOutput, calls=%fused_computation.10 | convolution fusion | flops 201375744 | bytes 25493504 | tf_op jit(solution)/shard_map/gcf,fd->gcd/dot_general | solution.py:103
  136.5 44.8 %all-gather.6.cloned.1.call-done = f32[32,2,6144]{2,1,0:T(2,128)} async-done(((f32[4,2,6144]{2,1,0:T(2,128)}), f32[32,2,6144]{2,1,0:T(2,128)}) %all-gather.6.cloned.1.call-update) | async-done | bytes 1572880 | tf_op jit(solution)/shard_map/all_gather | solution.py:14
  181.3 2.8 %reduce_sum.89 = f32[4,2,6144]{2,1,0:T(2,128)} reduce(f32[8,4,2,6144]{3,2,1,0:T(2,128)} %bitcast.73, f32[]{:T(128)} %constant.17.clone.1), dimensions={0}, to_apply=%region_11.12 | reduce | flops 344064 | bytes 1769476 | tf_op jit(solution)/shard_map/reduce_sum | solution.py:15
  184.1 3.4 %all-to-all-start.1 = ((f32[4,2,6144]{2,1,0:T(2,128)}), f32[4,2,6144]{2,1,0:T(2,128)S(1)}, u32[]{:S(2)}, u32[]{:S(2)}) async-start(f32[4,2,6144]{2,1,0:T(2,128)} %reduce_sum.89), calls=%async_computation.1 | async-start | bytes 393216 | tf_op jit(solution)/shard_map/all_to_all | solution.py:107
  187.5 5.3 %all-to-all-done.1 = f32[4,2,6144]{2,1,0:T(2,128)S(1)} async-done(((f32[4,2,6144]{2,1,0:T(2,128)}), f32[4,2,6144]{2,1,0:T(2,128)S(1)}, u32[]{:S(2)}, u32[]{:S(2)}) %all-to-all-start.1) | async-done | bytes 196640 | tf_op jit(solution)/shard_map/all_to_all | solution.py:107
  192.9 0.3 fusion.44
  193.2 0.6 dynamic-slice_convert_fusion
  (75 shorter events, 4.1 us)
Async XLA Ops:
  7.2 2.0 copy-start
  7.2 174.2 %all-gather.6.cloned.1.call-start = ((), (), s32[]{:S(2)}) async-start(), calls=%async_computation.2 | async-start | bytes 1769472 | tf_op jit(solution)/shard_map/all_gather | solution.py:14
  8.3 64.8 %copy-start.1 = (bf16[4,256,1024]{2,1,0:T(8,128)(2,1)S(1)}, bf16[4,256,1024]{2,1,0:T(8,128)(2,1)}, u32[]{:S(2)}) copy-start(bf16[4,256,1024]{2,1,0:T(8,128)(2,1)} %param.14) | copy-start | bytes 6291460
  73.0 32.2 %copy-start.4 = (s32[16,2]{0,1:T(2,128)S(1)}, s32[16,2]{0,1:T(2,128)}, u32[]{:S(2)}) copy-start(s32[16,2]{0,1:T(2,128)} %param.18) | copy-start | bytes 388
  106.3 3.4 %copy-start.3 = (f32[6144]{0:T(1024)S(1)}, f32[6144]{0:T(1024)}, u32[]{:S(2)}) copy-start(f32[6144]{0:T(1024)} %param.16) | copy-start | bytes 73732
  106.3 3.5 %copy-start.5 = (bf16[6144,4]{0,1:T(4,128)(2,1)S(1)}, bf16[6144,4]{0,1:T(4,128)(2,1)}, u32[]{:S(2)}) copy-start(bf16[6144,4]{0,1:T(4,128)(2,1)} %param.17) | copy-start | bytes 147460
  109.7 14.2 %copy-start.2 = (bf16[4,6144]{1,0:T(4,128)(2,1)}, bf16[4,6144]{1,0:T(4,128)(2,1)S(1)}, u32[]{:S(2)}) copy-start(bf16[4,6144]{1,0:T(4,128)(2,1)S(1)} %multiply_convert_fusion) | copy-start | bytes 147460
  184.1 8.7 %all-to-all-start.1 = ((f32[4,2,6144]{2,1,0:T(2,128)}), f32[4,2,6144]{2,1,0:T(2,128)S(1)}, u32[]{:S(2)}, u32[]{:S(2)}) async-start(f32[4,2,6144]{2,1,0:T(2,128)} %reduce_sum.89), calls=%async_computation.1 | async-start | bytes 393216 | tf_op jit(solution)/shard_map/all_to_all | solution.py:107
Sparse Core Ops, SparseCore 0:
  136.6 44.6 all-gather.5
